TPU v7x, 32 devices: a whole 2x2x4 slice. The times are simulated.
32 devices in a mesh: tensor: 4 (over x, core), replica: 4 (over z), fsdp: 2 (over y).
Axes of the slice: x: 2, y: 2, z: 4, core: 2. Of those that a mesh axis runs over, the one named last changes fastest.
Arguments:
- gradients: bfloat16 [4, 128, 28672], P('replica', 'fsdp', 'tensor'), may hold values from -6 to 6
- seeds: int32 [2], replicated, may hold values from 0 to 1073741823
- adam_step: int32 [1], replicated, may hold values from 1 to 8
- first_moment: float32 [128, 28672], P(('fsdp', 'replica'), 'tensor'), may hold values from -0.6 to 0.6
- second_moment: float32 [128, 28672], P(('fsdp', 'replica'), 'tensor'), may hold values from 0.001 to 0.1
Outputs:
- new_first: float32 [128, 28672], P(('fsdp', 'replica'), 'tensor')
- new_second: float32 [128, 28672], P(('fsdp', 'replica'), 'tensor')
- step_update: float32 [128, 28672], P(('fsdp', 'replica'), 'tensor')
All inputs are finite; a program needn't handle non-finite values.
Results may differ from a plain program's by a relative error of at most 0.012.
The roundings to bfloat16 on the way count: a program that leaves them out, or rounds other values in their place, can miss the bound.
Values may be sent and summed in bfloat16 or wider, within the bound.
No kernel may reach another device: no remote copies, remote signals or barrier semaphores. Data moves between devices by JAX's collectives and lax.ppermute only.
A program may use at most 64 MiB of HBM per device.

v0:
```python
import math
import jax
import jax.numpy as jnp
from jax import lax
from jax.sharding import PartitionSpec as P

RANK = 512


def scramble(value):
    value = value ^ lax.shift_right_logical(value, jnp.full_like(value, 16))
    value = value * jnp.int32(-2048144789)
    value = value ^ lax.shift_right_logical(value, jnp.full_like(value, 13))
    value = value * jnp.int32(-1028477387)
    value = value ^ lax.shift_right_logical(value, jnp.full_like(value, 16))
    return value


def projection_block(first_column, columns, rank, seeds):
    seed_key = seeds[0] ^ seeds[1] * jnp.int32(668265263)
    column = lax.broadcasted_iota(jnp.int32, (columns, rank), 0) + first_column
    entry = lax.broadcasted_iota(jnp.int32, (columns, rank), 1)
    counter = (column * jnp.int32(rank) + entry) * jnp.int32(2)
    hash_a = scramble(counter * jnp.int32(-1640531535) ^ seed_key)
    hash_b = scramble((counter + jnp.int32(1)) * jnp.int32(-1640531535) ^ seed_key)
    inverse = 1.0 / 16777216.0
    uniform_a = (
        lax.shift_right_logical(hash_a, jnp.full_like(hash_a, 8)).astype(jnp.float32) + 0.5
    ) * inverse
    uniform_b = (
        lax.shift_right_logical(hash_b, jnp.full_like(hash_b, 8)).astype(jnp.float32) + 0.5
    ) * inverse
    gauss = jnp.sqrt(-2.0 * jnp.log(uniform_a)) * jnp.cos(6.283185307179586 * uniform_b)
    return (gauss * rank ** (-0.5)).astype(jnp.bfloat16)


def per_device(gradients, seeds, adam_step, first_moment, second_moment):
    gradient = gradients[0]
    columns = gradient.shape[1]
    replicas = lax.axis_size("replica")
    column_start = lax.axis_index("tensor") * jnp.int32(columns)
    piece_cols = math.gcd(columns, 512)
    blocks = columns // piece_cols
    starts = column_start + lax.iota(jnp.int32, blocks) * jnp.int32(piece_cols)
    tiles = lax.map(lambda first: projection_block(first, piece_cols, RANK, seeds), starts)
    projection = tiles.reshape(columns, RANK)
    partial_value = jnp.dot(gradient, projection, preferred_element_type=jnp.float32) * (
        1.0 / replicas
    )
    share = lax.psum_scatter(partial_value, "replica", scatter_dimension=0, tiled=True)
    sketch = lax.psum(share, "tensor")
    sketch_rounded = sketch.astype(jnp.bfloat16)
    estimate = lax.dot_general(
        sketch_rounded, projection, (((1,), (1,)), ((), ())), preferred_element_type=jnp.float32
    )
    new_first = 0.9 * first_moment + 0.1 * estimate
    new_second = 0.95 * second_moment + 0.05 * estimate * estimate
    step_float = adam_step[0].astype(jnp.float32)
    fix_first = 1.0 - jnp.power(jnp.float32(0.9), step_float)
    fix_second = 1.0 - jnp.power(jnp.float32(0.95), step_float)
    step_update = new_first / fix_first / (jnp.sqrt(new_second / fix_second) + 1e-08)
    return (new_first, new_second, step_update)


def solution(mesh):
    placed = (
        P("replica", "fsdp", "tensor"),
        P(),
        P(),
        P(("fsdp", "replica"), "tensor"),
        P(("fsdp", "replica"), "tensor"),
    )
    return jax.shard_map(
        per_device,
        mesh=mesh,
        in_specs=placed,
        out_specs=(
            P(("fsdp", "replica"), "tensor"),
            P(("fsdp", "replica"), "tensor"),
            P(("fsdp", "replica"), "tensor"),
        ),
        check_vma=False,
    )
```

profile of v0, /device:TPU:1, one launch (start us, length us, event | category | flops | bytes accessed | tf_op | source)
XLA Modules:
  0.0 164.6 jit_solution(9987295474891056560)
XLA Ops:
  7.2 1.3 fusion.26
  9.9 99.4 %while.12 = (s32[]{:T(128)}, bf16[14,512,512]{2,1,0:T(8,128)(2,1)}, s32[14]{0:T(128)S(1)}, s32[]{:T(128)}, s32[]{:T(128)}) while((s32[]{:T(128)}, bf16[14,512,512]{2,1,0:T(8,128)(2,1)}, s32[14]{0:T(128)S(1)}, s32[]{:T(128)}, s32[]{:T(128)}) %tuple.33), condition=%wide.region_1.2_spmd, body=%wide.region_0.1_spmd.sunk | while | flops 9176066 | bytes 529485 | solution.py:45
  9.9 0.6 dynamic_slice.8
  10.5 0.6 add_multiply_fusion.2
  11.1 5.9 %fusion.31 = bf16[14,512,512]{2,1,0:T(8,128)(2,1)} fusion(bf16[14,512,512]{2,1,0:T(8,128)(2,1)} %get-tuple-element.105, s32[]{:T(128)} %get-tuple-element.104, s32[]{:T(128)} %get-tuple-element.112, s32[512]{0:T(512)S(1)} %add_multiply_fusion.2), kind=kLoop, calls=%fused_computation.25.clone.1 | loop fusion | flops 9175040 | bytes 527360 | tf_op jit(solution)/shard_map/while/body/jit(dynamic_update_index_in_dim)/dynamic_update_slice | solution.py:45
  17.0 0.6 dynamic_slice.8
  17.6 0.6 add_multiply_fusion.2
  18.2 5.9 %fusion.31 = bf16[14,512,512]{2,1,0:T(8,128)(2,1)} fusion(bf16[14,512,512]{2,1,0:T(8,128)(2,1)} %get-tuple-element.105, s32[]{:T(128)} %get-tuple-element.104, s32[]{:T(128)} %get-tuple-element.112, s32[512]{0:T(512)S(1)} %add_multiply_fusion.2), kind=kLoop, calls=%fused_computation.25.clone.1 | loop fusion | flops 9175040 | bytes 527360 | tf_op jit(solution)/shard_map/while/body/jit(dynamic_update_index_in_dim)/dynamic_update_slice | solution.py:45
  24.1 0.6 dynamic_slice.8
  24.7 0.6 add_multiply_fusion.2
  25.3 5.9 %fusion.31 = bf16[14,512,512]{2,1,0:T(8,128)(2,1)} fusion(bf16[14,512,512]{2,1,0:T(8,128)(2,1)} %get-tuple-element.105, s32[]{:T(128)} %get-tuple-element.104, s32[]{:T(128)} %get-tuple-element.112, s32[512]{0:T(512)S(1)} %add_multiply_fusion.2), kind=kLoop, calls=%fused_computation.25.clone.1 | loop fusion | flops 9175040 | bytes 527360 | tf_op jit(solution)/shard_map/while/body/jit(dynamic_update_index_in_dim)/dynamic_update_slice | solution.py:45
  31.2 0.6 dynamic_slice.8
  31.8 0.6 add_multiply_fusion.2
  32.4 5.9 %fusion.31 = bf16[14,512,512]{2,1,0:T(8,128)(2,1)} fusion(bf16[14,512,512]{2,1,0:T(8,128)(2,1)} %get-tuple-element.105, s32[]{:T(128)} %get-tuple-element.104, s32[]{:T(128)} %get-tuple-element.112, s32[512]{0:T(512)S(1)} %add_multiply_fusion.2), kind=kLoop, calls=%fused_computation.25.clone.1 | loop fusion | flops 9175040 | bytes 527360 | tf_op jit(solution)/shard_map/while/body/jit(dynamic_update_index_in_dim)/dynamic_update_slice | solution.py:45
  38.3 0.6 dynamic_slice.8
  38.9 0.6 add_multiply_fusion.2
  39.5 5.8 %fusion.31 = bf16[14,512,512]{2,1,0:T(8,128)(2,1)} fusion(bf16[14,512,512]{2,1,0:T(8,128)(2,1)} %get-tuple-element.105, s32[]{:T(128)} %get-tuple-element.104, s32[]{:T(128)} %get-tuple-element.112, s32[512]{0:T(512)S(1)} %add_multiply_fusion.2), kind=kLoop, calls=%fused_computation.25.clone.1 | loop fusion | flops 9175040 | bytes 527360 | tf_op jit(solution)/shard_map/while/body/jit(dynamic_update_index_in_dim)/dynamic_update_slice | solution.py:45
  45.4 0.6 dynamic_slice.8
  46.0 0.6 add_multiply_fusion.2
  46.6 5.9 %fusion.31 = bf16[14,512,512]{2,1,0:T(8,128)(2,1)} fusion(bf16[14,512,512]{2,1,0:T(8,128)(2,1)} %get-tuple-element.105, s32[]{:T(128)} %get-tuple-element.104, s32[]{:T(128)} %get-tuple-element.112, s32[512]{0:T(512)S(1)} %add_multiply_fusion.2), kind=kLoop, calls=%fused_computation.25.clone.1 | loop fusion | flops 9175040 | bytes 527360 | tf_op jit(solution)/shard_map/while/body/jit(dynamic_update_index_in_dim)/dynamic_update_slice | solution.py:45
  52.5 0.6 dynamic_slice.8
  53.0 0.6 add_multiply_fusion.2
  53.7 5.9 %fusion.31 = bf16[14,512,512]{2,1,0:T(8,128)(2,1)} fusion(bf16[14,512,512]{2,1,0:T(8,128)(2,1)} %get-tuple-element.105, s32[]{:T(128)} %get-tuple-element.104, s32[]{:T(128)} %get-tuple-element.112, s32[512]{0:T(512)S(1)} %add_multiply_fusion.2), kind=kLoop, calls=%fused_computation.25.clone.1 | loop fusion | flops 9175040 | bytes 527360 | tf_op jit(solution)/shard_map/while/body/jit(dynamic_update_index_in_dim)/dynamic_update_slice | solution.py:45
  59.6 0.6 dynamic_slice.8
  60.1 0.6 add_multiply_fusion.2
  60.8 5.9 %fusion.31 = bf16[14,512,512]{2,1,0:T(8,128)(2,1)} fusion(bf16[14,512,512]{2,1,0:T(8,128)(2,1)} %get-tuple-element.105, s32[]{:T(128)} %get-tuple-element.104, s32[]{:T(128)} %get-tuple-element.112, s32[512]{0:T(512)S(1)} %add_multiply_fusion.2), kind=kLoop, calls=%fused_computation.25.clone.1 | loop fusion | flops 9175040 | bytes 527360 | tf_op jit(solution)/shard_map/while/body/jit(dynamic_update_index_in_dim)/dynamic_update_slice | solution.py:45
  66.7 0.6 dynamic_slice.8
  67.2 0.6 add_multiply_fusion.2
  67.9 5.9 %fusion.31 = bf16[14,512,512]{2,1,0:T(8,128)(2,1)} fusion(bf16[14,512,512]{2,1,0:T(8,128)(2,1)} %get-tuple-element.105, s32[]{:T(128)} %get-tuple-element.104, s32[]{:T(128)} %get-tuple-element.112, s32[512]{0:T(512)S(1)} %add_multiply_fusion.2), kind=kLoop, calls=%fused_computation.25.clone.1 | loop fusion | flops 9175040 | bytes 527360 | tf_op jit(solution)/shard_map/while/body/jit(dynamic_update_index_in_dim)/dynamic_update_slice | solution.py:45
  73.8 0.6 dynamic_slice.8
  74.3 0.6 add_multiply_fusion.2
  75.0 5.9 %fusion.31 = bf16[14,512,512]{2,1,0:T(8,128)(2,1)} fusion(bf16[14,512,512]{2,1,0:T(8,128)(2,1)} %get-tuple-element.105, s32[]{:T(128)} %get-tuple-element.104, s32[]{:T(128)} %get-tuple-element.112, s32[512]{0:T(512)S(1)} %add_multiply_fusion.2), kind=kLoop, calls=%fused_computation.25.clone.1 | loop fusion | flops 9175040 | bytes 527360 | tf_op jit(solution)/shard_map/while/body/jit(dynamic_update_index_in_dim)/dynamic_update_slice | solution.py:45
  80.9 0.6 dynamic_slice.8
  81.4 0.6 add_multiply_fusion.2
  82.1 5.9 %fusion.31 = bf16[14,512,512]{2,1,0:T(8,128)(2,1)} fusion(bf16[14,512,512]{2,1,0:T(8,128)(2,1)} %get-tuple-element.105, s32[]{:T(128)} %get-tuple-element.104, s32[]{:T(128)} %get-tuple-element.112, s32[512]{0:T(512)S(1)} %add_multiply_fusion.2), kind=kLoop, calls=%fused_computation.25.clone.1 | loop fusion | flops 9175040 | bytes 527360 | tf_op jit(solution)/shard_map/while/body/jit(dynamic_update_index_in_dim)/dynamic_update_slice | solution.py:45
  88.5 0.6 add_multiply_fusion.2
  89.2 5.9 %fusion.31 = bf16[14,512,512]{2,1,0:T(8,128)(2,1)} fusion(bf16[14,512,512]{2,1,0:T(8,128)(2,1)} %get-tuple-element.105, s32[]{:T(128)} %get-tuple-element.104, s32[]{:T(128)} %get-tuple-element.112, s32[512]{0:T(512)S(1)} %add_multiply_fusion.2), kind=kLoop, calls=%fused_computation.25.clone.1 | loop fusion | flops 9175040 | bytes 527360 | tf_op jit(solution)/shard_map/while/body/jit(dynamic_update_index_in_dim)/dynamic_update_slice | solution.py:45
  95.1 0.6 dynamic_slice.8
  95.6 0.6 add_multiply_fusion.2
  96.3 5.9 %fusion.31 = bf16[14,512,512]{2,1,0:T(8,128)(2,1)} fusion(bf16[14,512,512]{2,1,0:T(8,128)(2,1)} %get-tuple-element.105, s32[]{:T(128)} %get-tuple-element.104, s32[]{:T(128)} %get-tuple-element.112, s32[512]{0:T(512)S(1)} %add_multiply_fusion.2), kind=kLoop, calls=%fused_computation.25.clone.1 | loop fusion | flops 9175040 | bytes 527360 | tf_op jit(solution)/shard_map/while/body/jit(dynamic_update_index_in_dim)/dynamic_update_slice | solution.py:45
  102.7 0.6 add_multiply_fusion.2
  103.4 5.9 %fusion.31 = bf16[14,512,512]{2,1,0:T(8,128)(2,1)} fusion(bf16[14,512,512]{2,1,0:T(8,128)(2,1)} %get-tuple-element.105, s32[]{:T(128)} %get-tuple-element.104, s32[]{:T(128)} %get-tuple-element.112, s32[512]{0:T(512)S(1)} %add_multiply_fusion.2), kind=kLoop, calls=%fused_computation.25.clone.1 | loop fusion | flops 9175040 | bytes 527360 | tf_op jit(solution)/shard_map/while/body/jit(dynamic_update_index_in_dim)/dynamic_update_slice | solution.py:45
  109.2 5.2 %fusion.20 = f32[64,512]{0,1:T(8,128)S(1)} fusion(bf16[7168,512]{1,0:T(8,128)(2,1)} %bitcast.16, bf16[1,64,7168]{2,1,0:T(8,128)(2,1)S(1)} %copy-done), kind=kOutput, calls=%fused_computation.28 | convolution fusion | flops 469794816 | bytes 8388608 | tf_op jit(solution)/shard_map/dot_general | solution.py:47
  114.4 0.8 copy.8
  116.0 18.6 %reduce-scatter.4.cloned.1.call-done = f32[16,512]{1,0:T(8,128)} async-done(((f32[64,512]{1,0:T(8,128)}), f32[16,512]{1,0:T(8,128)}) %reduce-scatter.4.cloned.1.call-update) | async-done | bytes 32784
  134.5 0.9 copy.9
  135.4 16.2 %psum.7 = bf16[16,512]{0,1:T(8,128)(2,1)S(1)} all-reduce(f32[16,512]{0,1:T(8,128)S(1)} %copy.9), channel_id=1, replica_groups=mesh['tensor'=4,'replica'=4,'fsdp'=2] {'tensor'}, use_global_device_ids=true, to_apply=%region_3.4 | all-reduce | flops 8192 | bytes 49152 | tf_op jit(solution)/shard_map/psum | solution.py:51
  151.6 6.2 %multiply_divide_fusion = (f32[16,7168]{1,0:T(8,128)}, f32[16,7168]{1,0:T(8,128)}, f32[16,7168]{1,0:T(8,128)}) fusion(f32[]{:T(128)} %bitcast.6, f32[]{:T(128)} %bitcast.5, f32[16,7168]{1,0:T(8,128)S(1)} %copy-done.1, f32[16,7168]{1,0:T(8,128)S(1)} %copy-done.2, bf16[16,512]{0,1:T(8,128)(2,1)S(1)} %psum.7, bf16[7168,512]{1,0:T(8,128)(2,1)} %bitcast.17), kind=kOutput, calls=%fused_computation.32 | convolution fusion | flops 118702080 | bytes 9650184 | tf_op jit(solution)/shard_map/dot_general | solution.py:53
  (12 shorter events, 1.2 us)
Async XLA Ops:
  7.2 102.1 %copy-start = (bf16[1,64,7168]{2,1,0:T(8,128)(2,1)S(1)}, bf16[1,64,7168]{2,1,0:T(8,128)(2,1)}, u32[]{:S(2)}) copy-start(bf16[1,64,7168]{2,1,0:T(8,128)(2,1)} %param.7) | copy-start | bytes 2752516
  7.2 127.3 %reduce-scatter.4.cloned.1.call-start = ((), (), s32[]{:S(2)}) async-start(), calls=%async_computation.1 | async-start | bytes 163840
  9.9 141.7 %copy-start.1 = (f32[16,7168]{1,0:T(8,128)S(1)}, f32[16,7168]{1,0:T(8,128)}, u32[]{:S(2)}) copy-start(f32[16,7168]{1,0:T(8,128)} %param.11) | copy-start | bytes 1376260
  9.9 141.7 %copy-start.2 = (f32[16,7168]{1,0:T(8,128)S(1)}, f32[16,7168]{1,0:T(8,128)}, u32[]{:S(2)}) copy-start(f32[16,7168]{1,0:T(8,128)} %param.10) | copy-start | bytes 1376260
Sparse Core Ops, SparseCore 0:
  115.3 19.1 reduce-scatter.3
where the time goes:
time: 165 us
  other arithmetic  91.1 us (55%)
  waiting for transfers between devices  18.6 us (11%)
  blocking collectives  16.2 us (10%)
  between operations  16.1 us (10%)
  matrix products  11.4 us (7%)
  local copies, waits for them, and re-layouts  11.2 us (7%)
    dynamic_update_slice x14, other arithmetic, per_device(): lax.map(lambda first: projection_block(first, piece_cols, RANK, seeds), s...  82 us
    unnamed x2, waiting for transfers between devices  18.6 us
    psum x1, blocking collectives, per_device(): sketch = lax.psum(share, 'tensor')  16.2 us
    mul x14, other arithmetic, projection_block(): counter = (column * jnp.int32(rank) + entry) * jnp.int32(2)  9.07 us
    dynamic_slice x14, local copies, waits for them, and re-layouts, per_device(): lax.map(lambda first: projection_block(first, piece_cols, RANK, seeds), s...  8.15 us
    dot_general x1, matrix products, per_device(): lax.dot_general(sketch_rounded, projection, (((1,), (1,)), ((), ())), pre...  6.19 us
    dot_general x1, matrix products, per_device(): jnp.dot(gradient, projection, preferred_element_type=jnp.float32)  5.17 us
  transfers between devices with their start and end apart: 1, of which 1 were waited for; matrix products, arithmetic and copies ran while one was open for 0% of the time, Pallas kernels for 0%

commit v1 on v0

--- a/solution.py
+++ b/solution.py
@@ -48,7 +48,7 @@
         1.0 / replicas
     )
     share = lax.psum_scatter(partial_value, "replica", scatter_dimension=0, tiled=True)
-    sketch = lax.psum(share, "tensor")
+    sketch = jnp.sum(lax.all_gather(share, "tensor"), axis=0)
     sketch_rounded = sketch.astype(jnp.bfloat16)
     estimate = lax.dot_general(
         sketch_rounded, projection, (((1,), (1,)), ((), ())), preferred_element_type=jnp.float32

time: 165 us -> 156 us (0.945)
  blocking collectives: 16.2 us -> 8.49 us
  local copies, waits for them, and re-layouts: 11.2 us -> 9.49 us
    reduce_scatter x0 -> x1, waiting for transfers between devices: none -> 18.6 us  [per_device(): lax.psum_scatter(partial_value, 'replica', scatter_dimension=0, tiled=True)]
    unnamed x2 -> x1, waiting for transfers between devices: 18.6 us -> 0.02 us
    psum x1 -> x0, blocking collectives: 16.2 us -> none  [per_device(): sketch = lax.psum(share, 'tensor')]
    all_gather x0 -> x1, blocking collectives: none -> 8.49 us  [per_device(): sketch = jnp.sum(lax.all_gather(share, 'tensor'), axis=0)]
    unnamed x8 -> x6, local copies, waits for them, and re-layouts: 1.67 us -> 0.02 us
where the time goes in v1:
time: 156 us; the launch traced here: 155 us
  other arithmetic  91.1 us (58%)
  waiting for transfers between devices  18.6 us (12%)
  between operations  16.1 us (10%)
  matrix products  11.4 us (7%)
  local copies, waits for them, and re-layouts  9.49 us (6%)
  blocking collectives  8.49 us (5%)
    dynamic_update_slice x14, other arithmetic, per_device(): lax.map(lambda first: projection_block(first, piece_cols, RANK, seeds), s...  82 us
    reduce_scatter x1, waiting for transfers between devices, per_device(): lax.psum_scatter(partial_value, 'replica', scatter_dimension=0, tiled=True)  18.6 us
    mul x14, other arithmetic, projection_block(): counter = (column * jnp.int32(rank) + entry) * jnp.int32(2)  9.07 us
    all_gather x1, blocking collectives, per_device(): sketch = jnp.sum(lax.all_gather(share, 'tensor'), axis=0)  8.49 us
    dynamic_slice x14, local copies, waits for them, and re-layouts, per_device(): lax.map(lambda first: projection_block(first, piece_cols, RANK, seeds), s...  8.15 us
    dot_general x1, matrix products, per_device(): lax.dot_general(sketch_rounded, projection, (((1,), (1,)), ((), ())), pre...  6.19 us
    dot_general x1, matrix products, per_device(): jnp.dot(gradient, projection, preferred_element_type=jnp.float32)  5.2 us
  transfers between devices with their start and end apart: 1, of which 1 were waited for; matrix products, arithmetic and copies ran while one was open for 0% of the time, Pallas kernels for 0%

profile of v1, /device:TPU:1, one launch (start us, length us, event | category | flops | bytes accessed | tf_op | source)
XLA Modules:
  0.0 155.3 jit_solution(15997003003464879319)
XLA Ops:
  7.2 1.3 fusion.26
  9.9 99.4 %while.12 = (s32[]{:T(128)}, bf16[14,512,512]{2,1,0:T(8,128)(2,1)}, s32[14]{0:T(128)S(1)}, s32[]{:T(128)}, s32[]{:T(128)}) while((s32[]{:T(128)}, bf16[14,512,512]{2,1,0:T(8,128)(2,1)}, s32[14]{0:T(128)S(1)}, s32[]{:T(128)}, s32[]{:T(128)}) %tuple.33), condition=%wide.region_1.2_spmd, body=%wide.region_0.1_spmd.sunk | while | flops 9176066 | bytes 529485 | solution.py:45
  9.9 0.6 dynamic_slice.8
  10.5 0.6 add_multiply_fusion.2
  11.1 5.9 %fusion.31 = bf16[14,512,512]{2,1,0:T(8,128)(2,1)} fusion(bf16[14,512,512]{2,1,0:T(8,128)(2,1)} %get-tuple-element.105, s32[]{:T(128)} %get-tuple-element.104, s32[]{:T(128)} %get-tuple-element.112, s32[512]{0:T(512)S(1)} %add_multiply_fusion.2), kind=kLoop, calls=%fused_computation.25.clone.1 | loop fusion | flops 9175040 | bytes 527360 | tf_op jit(solution)/shard_map/while/body/jit(dynamic_update_index_in_dim)/dynamic_update_slice | solution.py:45
  17.0 0.6 dynamic_slice.8
  17.6 0.6 add_multiply_fusion.2
  18.2 5.9 %fusion.31 = bf16[14,512,512]{2,1,0:T(8,128)(2,1)} fusion(bf16[14,512,512]{2,1,0:T(8,128)(2,1)} %get-tuple-element.105, s32[]{:T(128)} %get-tuple-element.104, s32[]{:T(128)} %get-tuple-element.112, s32[512]{0:T(512)S(1)} %add_multiply_fusion.2), kind=kLoop, calls=%fused_computation.25.clone.1 | loop fusion | flops 9175040 | bytes 527360 | tf_op jit(solution)/shard_map/while/body/jit(dynamic_update_index_in_dim)/dynamic_update_slice | solution.py:45
  24.1 0.6 dynamic_slice.8
  24.7 0.6 add_multiply_fusion.2
  25.3 5.9 %fusion.31 = bf16[14,512,512]{2,1,0:T(8,128)(2,1)} fusion(bf16[14,512,512]{2,1,0:T(8,128)(2,1)} %get-tuple-element.105, s32[]{:T(128)} %get-tuple-element.104, s32[]{:T(128)} %get-tuple-element.112, s32[512]{0:T(512)S(1)} %add_multiply_fusion.2), kind=kLoop, calls=%fused_computation.25.clone.1 | loop fusion | flops 9175040 | bytes 527360 | tf_op jit(solution)/shard_map/while/body/jit(dynamic_update_index_in_dim)/dynamic_update_slice | solution.py:45
  31.2 0.6 dynamic_slice.8
  31.7 0.6 add_multiply_fusion.2
  32.4 5.9 %fusion.31 = bf16[14,512,512]{2,1,0:T(8,128)(2,1)} fusion(bf16[14,512,512]{2,1,0:T(8,128)(2,1)} %get-tuple-element.105, s32[]{:T(128)} %get-tuple-element.104, s32[]{:T(128)} %get-tuple-element.112, s32[512]{0:T(512)S(1)} %add_multiply_fusion.2), kind=kLoop, calls=%fused_computation.25.clone.1 | loop fusion | flops 9175040 | bytes 527360 | tf_op jit(solution)/shard_map/while/body/jit(dynamic_update_index_in_dim)/dynamic_update_slice | solution.py:45
  38.3 0.6 dynamic_slice.8
  38.8 0.6 add_multiply_fusion.2
  39.5 5.8 %fusion.31 = bf16[14,512,512]{2,1,0:T(8,128)(2,1)} fusion(bf16[14,512,512]{2,1,0:T(8,128)(2,1)} %get-tuple-element.105, s32[]{:T(128)} %get-tuple-element.104, s32[]{:T(128)} %get-tuple-element.112, s32[512]{0:T(512)S(1)} %add_multiply_fusion.2), kind=kLoop, calls=%fused_computation.25.clone.1 | loop fusion | flops 9175040 | bytes 527360 | tf_op jit(solution)/shard_map/while/body/jit(dynamic_update_index_in_dim)/dynamic_update_slice | solution.py:45
  45.3 0.6 dynamic_slice.8
  45.9 0.6 add_multiply_fusion.2
  46.6 5.9 %fusion.31 = bf16[14,512,512]{2,1,0:T(8,128)(2,1)} fusion(bf16[14,512,512]{2,1,0:T(8,128)(2,1)} %get-tuple-element.105, s32[]{:T(128)} %get-tuple-element.104, s32[]{:T(128)} %get-tuple-element.112, s32[512]{0:T(512)S(1)} %add_multiply_fusion.2), kind=kLoop, calls=%fused_computation.25.clone.1 | loop fusion | flops 9175040 | bytes 527360 | tf_op jit(solution)/shard_map/while/body/jit(dynamic_update_index_in_dim)/dynamic_update_slice | solution.py:45
  52.4 0.6 dynamic_slice.8
  53.0 0.6 add_multiply_fusion.2
  53.7 5.9 %fusion.31 = bf16[14,512,512]{2,1,0:T(8,128)(2,1)} fusion(bf16[14,512,512]{2,1,0:T(8,128)(2,1)} %get-tuple-element.105, s32[]{:T(128)} %get-tuple-element.104, s32[]{:T(128)} %get-tuple-element.112, s32[512]{0:T(512)S(1)} %add_multiply_fusion.2), kind=kLoop, calls=%fused_computation.25.clone.1 | loop fusion | flops 9175040 | bytes 527360 | tf_op jit(solution)/shard_map/while/body/jit(dynamic_update_index_in_dim)/dynamic_update_slice | solution.py:45
  59.5 0.6 dynamic_slice.8
  60.1 0.6 add_multiply_fusion.2
  60.8 5.9 %fusion.31 = bf16[14,512,512]{2,1,0:T(8,128)(2,1)} fusion(bf16[14,512,512]{2,1,0:T(8,128)(2,1)} %get-tuple-element.105, s32[]{:T(128)} %get-tuple-element.104, s32[]{:T(128)} %get-tuple-element.112, s32[512]{0:T(512)S(1)} %add_multiply_fusion.2), kind=kLoop, calls=%fused_computation.25.clone.1 | loop fusion | flops 9175040 | bytes 527360 | tf_op jit(solution)/shard_map/while/body/jit(dynamic_update_index_in_dim)/dynamic_update_slice | solution.py:45
  66.6 0.6 dynamic_slice.8
  67.2 0.6 add_multiply_fusion.2
  67.9 5.9 %fusion.31 = bf16[14,512,512]{2,1,0:T(8,128)(2,1)} fusion(bf16[14,512,512]{2,1,0:T(8,128)(2,1)} %get-tuple-element.105, s32[]{:T(128)} %get-tuple-element.104, s32[]{:T(128)} %get-tuple-element.112, s32[512]{0:T(512)S(1)} %add_multiply_fusion.2), kind=kLoop, calls=%fused_computation.25.clone.1 | loop fusion | flops 9175040 | bytes 527360 | tf_op jit(solution)/shard_map/while/body/jit(dynamic_update_index_in_dim)/dynamic_update_slice | solution.py:45
  73.7 0.6 dynamic_slice.8
  74.3 0.6 add_multiply_fusion.2
  75.0 5.9 %fusion.31 = bf16[14,512,512]{2,1,0:T(8,128)(2,1)} fusion(bf16[14,512,512]{2,1,0:T(8,128)(2,1)} %get-tuple-element.105, s32[]{:T(128)} %get-tuple-element.104, s32[]{:T(128)} %get-tuple-element.112, s32[512]{0:T(512)S(1)} %add_multiply_fusion.2), kind=kLoop, calls=%fused_computation.25.clone.1 | loop fusion | flops 9175040 | bytes 527360 | tf_op jit(solution)/shard_map/while/body/jit(dynamic_update_index_in_dim)/dynamic_update_slice | solution.py:45
  80.8 0.6 dynamic_slice.8
  81.4 0.6 add_multiply_fusion.2
  82.1 5.9 %fusion.31 = bf16[14,512,512]{2,1,0:T(8,128)(2,1)} fusion(bf16[14,512,512]{2,1,0:T(8,128)(2,1)} %get-tuple-element.105, s32[]{:T(128)} %get-tuple-element.104, s32[]{:T(128)} %get-tuple-element.112, s32[512]{0:T(512)S(1)} %add_multiply_fusion.2), kind=kLoop, calls=%fused_computation.25.clone.1 | loop fusion | flops 9175040 | bytes 527360 | tf_op jit(solution)/shard_map/while/body/jit(dynamic_update_index_in_dim)/dynamic_update_slice | solution.py:45
  87.9 0.6 dynamic_slice.8
  88.5 0.6 add_multiply_fusion.2
  89.2 5.9 %fusion.31 = bf16[14,512,512]{2,1,0:T(8,128)(2,1)} fusion(bf16[14,512,512]{2,1,0:T(8,128)(2,1)} %get-tuple-element.105, s32[]{:T(128)} %get-tuple-element.104, s32[]{:T(128)} %get-tuple-element.112, s32[512]{0:T(512)S(1)} %add_multiply_fusion.2), kind=kLoop, calls=%fused_computation.25.clone.1 | loop fusion | flops 9175040 | bytes 527360 | tf_op jit(solution)/shard_map/while/body/jit(dynamic_update_index_in_dim)/dynamic_update_slice | solution.py:45
  95.0 0.6 dynamic_slice.8
  95.6 0.6 add_multiply_fusion.2
  96.3 5.9 %fusion.31 = bf16[14,512,512]{2,1,0:T(8,128)(2,1)} fusion(bf16[14,512,512]{2,1,0:T(8,128)(2,1)} %get-tuple-element.105, s32[]{:T(128)} %get-tuple-element.104, s32[]{:T(128)} %get-tuple-element.112, s32[512]{0:T(512)S(1)} %add_multiply_fusion.2), kind=kLoop, calls=%fused_computation.25.clone.1 | loop fusion | flops 9175040 | bytes 527360 | tf_op jit(solution)/shard_map/while/body/jit(dynamic_update_index_in_dim)/dynamic_update_slice | solution.py:45
  102.1 0.6 dynamic_slice.8
  102.7 0.6 add_multiply_fusion.2
  103.4 5.9 %fusion.31 = bf16[14,512,512]{2,1,0:T(8,128)(2,1)} fusion(bf16[14,512,512]{2,1,0:T(8,128)(2,1)} %get-tuple-element.105, s32[]{:T(128)} %get-tuple-element.104, s32[]{:T(128)} %get-tuple-element.112, s32[512]{0:T(512)S(1)} %add_multiply_fusion.2), kind=kLoop, calls=%fused_computation.25.clone.1 | loop fusion | flops 9175040 | bytes 527360 | tf_op jit(solution)/shard_map/while/body/jit(dynamic_update_index_in_dim)/dynamic_update_slice | solution.py:45
  109.2 5.2 %fusion.20 = f32[64,512]{1,0:T(8,128)} fusion(bf16[7168,512]{1,0:T(8,128)(2,1)} %bitcast.16, bf16[1,64,7168]{2,1,0:T(8,128)(2,1)S(1)} %copy-done), kind=kOutput, calls=%fused_computation.28 | convolution fusion | flops 469794816 | bytes 8388608 | tf_op jit(solution)/shard_map/dot_general | solution.py:47
  115.2 18.6 %reduce-scatter.2.cloned.1.call-done = f32[16,512]{1,0:T(8,128)} async-done(((f32[64,512]{1,0:T(8,128)}), f32[16,512]{1,0:T(8,128)}) %reduce-scatter.2.cloned.1.call-update) | async-done | bytes 32784 | tf_op jit(solution)/shard_map/reduce_scatter | solution.py:50
  133.7 8.5 %all-gather = f32[64,512]{1,0:T(8,128)S(1)} all-gather(f32[16,512]{1,0:T(8,128)} %reduce-scatter.2.cloned.1.call-done), channel_id=2, replica_groups=mesh['tensor'=4,'replica'=4,'fsdp'=2] {'tensor'}, dimensions={0}, use_global_device_ids=true | all-gather | bytes 163840 | tf_op jit(solution)/shard_map/all_gather | solution.py:51
  142.3 6.2 %multiply_divide_fusion = (f32[16,7168]{1,0:T(8,128)}, f32[16,7168]{1,0:T(8,128)}, f32[16,7168]{1,0:T(8,128)}) fusion(f32[]{:T(128)} %bitcast.7, f32[]{:T(128)} %bitcast.6, f32[16,7168]{1,0:T(8,128)S(1)} %copy-done.1, f32[16,7168]{1,0:T(8,128)S(1)} %copy-done.2, bf16[16,512]{1,0:T(8,128)(2,1)S(1)} %reduce_sum.9, bf16[7168,512]{1,0:T(8,128)(2,1)} %bitcast.17), kind=kOutput, calls=%fused_computation.32 | convolution fusion | flops 118702080 | bytes 9650184 | tf_op jit(solution)/shard_map/dot_general | solution.py:53
  (11 shorter events, 0.1 us)
Async XLA Ops:
  7.2 102.1 %copy-start = (bf16[1,64,7168]{2,1,0:T(8,128)(2,1)S(1)}, bf16[1,64,7168]{2,1,0:T(8,128)(2,1)}, u32[]{:S(2)}) copy-start(bf16[1,64,7168]{2,1,0:T(8,128)(2,1)} %param.7) | copy-start | bytes 2752516
  7.2 126.6 %reduce-scatter.2.cloned.1.call-start = ((), (), s32[]{:S(2)}) async-start(), calls=%async_computation.1 | async-start | bytes 163840 | tf_op jit(solution)/shard_map/reduce_scatter | solution.py:50
  109.2 33.0 %copy-start.1 = (f32[16,7168]{1,0:T(8,128)S(1)}, f32[16,7168]{1,0:T(8,128)}, u32[]{:S(2)}) copy-start(f32[16,7168]{1,0:T(8,128)} %param.11) | copy-start | bytes 1376260
  109.2 33.0 %copy-start.2 = (f32[16,7168]{1,0:T(8,128)S(1)}, f32[16,7168]{1,0:T(8,128)}, u32[]{:S(2)}) copy-start(f32[16,7168]{1,0:T(8,128)} %param.10) | copy-start | bytes 1376260
Sparse Core Ops, SparseCore 0:
  114.6 19.1 reduce-scatter.1
